TPU v7x, 32 devices: a whole 2x2x4 slice. The times are simulated.
32 devices in a mesh: parts: 2 (over y), tm: 4 (over x, core), cols: 4 (over z).
Axes of the slice: x: 2, y: 2, z: 4, core: 2. Of those that a mesh axis runs over, the one named last changes fastest.
Arguments:
- noise: float32 [16, 1024, 1024], P(('parts', 'tm'), None, 'cols'), parts along dimension 0, may hold values from -6 to 6
- inv_diag: float32 [16, 1024, 1024], P(('parts', 'tm'), None, 'cols'), parts along dimension 0, may hold values from -2 to 2, as said below
- coupling: float32 [16, 1024, 1024], P(('parts', 'tm'), None, 'cols'), parts along dimension 0, may hold values from -1 to 1, as said below
- order: int32 [1024], replicated, may hold values from 0 to 1023, each once
Outputs:
- sample: float32 [16, 1024, 1024], P(('parts', 'tm'), None, 'cols'), parts along dimension 0
There are 2 independent parts, one for each index of `parts`. A program takes and returns all parts, laid end to end along the dimension named above; an argument that names none is the same for every part. Nothing has to cross between parts.
Inputs may be any that keep to these rules, and one draw needn't show every extreme that they name: `order`: each of 0 to 1023 appears once. `inv_diag`: diagonal entries lie between 0.5 and 2, off-diagonal entries are small in magnitude. `coupling`: diagonal entries lie between 0.5 and 0.97, off-diagonal entries are small in magnitude.
All inputs are finite; a program needn't handle non-finite values.
Results may differ from a plain program's by a relative error of at most 0.00013.
Values sent between devices are 32-bit elements; how exact they have to be, the bound alone decides.
No kernel may reach another device: no remote copies, remote signals or barrier semaphores. Data moves between devices by JAX's collectives and lax.ppermute only.
A program may use at most 128 MiB of HBM per device.

v0:
```python
import jax
import jax.numpy as jnp
from jax import lax
from jax.sharding import PartitionSpec as P

precise = lax.Precision.HIGHEST


def shifted(block, axis, distance):
    devices = range(lax.axis_size(axis))
    route = [(i - distance, i) for i in devices if i - distance in devices]
    return lax.ppermute(block, axis, route)


def fold_with(operand, segment):
    return jnp.dot(segment, operand, precision=precise, preferred_element_type=jnp.float32)


def shards(noise, inv_diag, coupling, order):
    block_count = noise.shape[0]
    sample_count = noise.shape[2]
    driven = jnp.einsum(
        "kmn,kns->kms",
        lax.all_gather(inv_diag, "cols", axis=2, tiled=True),
        noise,
        precision=precise,
        preferred_element_type=jnp.float32,
    )
    local_field = driven[block_count - 1]
    reduced = coupling[block_count - 1]
    block = 0
    operand = jnp.concatenate([local_field, reduced], axis=1)
    product = fold_with(operand, lax.all_gather(coupling[block], "cols", axis=1, tiled=True))
    local_field = driven[block] + product[:, :sample_count]
    reduced = product[:, sample_count:]
    reduced_full = lax.all_gather(reduced, "cols", axis=1, tiled=True)

    def relay_step(step, carry):
        current, incoming = carry
        incoming = shifted(current, "tm", -1)
        current = local_field + jnp.dot(
            reduced_full, incoming, precision=precise, preferred_element_type=jnp.float32
        )
        return (current, incoming)

    _, entering = lax.fori_loop(
        0, lax.axis_size("tm"), relay_step, (local_field, jnp.zeros_like(local_field))
    )
    carried = entering
    results = [None] * block_count
    for block in range(block_count - 1, -1, -1):
        product = fold_with(carried, lax.all_gather(coupling[block], "cols", axis=1, tiled=True))
        carried = driven[block] + product
        results[block] = carried
    stacked = jnp.stack(results, axis=0)
    return jnp.take(stacked, order, axis=1)


def solution(mesh):
    return jax.shard_map(
        shards,
        mesh=mesh,
        in_specs=(
            P(("parts", "tm"), None, "cols"),
            P(("parts", "tm"), None, "cols"),
            P(("parts", "tm"), None, "cols"),
            P(),
        ),
        out_specs=P(("parts", "tm"), None, "cols"),
        check_vma=False,
    )
```

profile of v0, /device:TPU:1, one launch (start us, length us, event | category | flops | bytes accessed | tf_op | source)
XLA Modules:
  0.0 545.5 jit_solution(10568745071062961867)
XLA Ops:
  7.3 3.1 fusion.32
  10.4 1.6 copy.19
  12.0 148.9 %all-gather.7.cloned.1.call-done = f32[2,1024,1024]{2,1,0:T(8,128)} async-done(((f32[2,1024,256]{2,1,0:T(8,128)}), f32[2,1024,1024]{2,1,0:T(8,128)}) %all-gather.7.cloned.1.call-update) | async-done | bytes 8388624 | tf_op jit(solution)/shard_map/all_gather | solution.py:24
  160.9 9.8 %fusion.33 = f32[2,1024,256]{1,2,0:T(8,128)S(1)} fusion(f32[2,1024,1024]{2,1,0:T(8,128)} %all-gather.7.cloned.1.call-done, f32[2,1024,256]{2,1,0:T(8,128)S(1)} %copy-done), kind=kOutput, calls=%fused_computation.28 | convolution fusion | flops 6442450944 | bytes 12582912 | tf_op jit(solution)/shard_map/kmn,kns->kms/dot_general | solution.py:22
  170.7 1.3 copy-done.1
  173.1 68.1 %all-gather.11.cloned.1.call-done = f32[1,1024,1024]{2,1,0:T(8,128)} async-done(((f32[1,1024,256]{2,1,0:T(8,128)}), f32[1,1024,1024]{2,1,0:T(8,128)}) %all-gather.11.cloned.1.call-update) | async-done | bytes 4194320 | tf_op jit(solution)/shard_map/all_gather | solution.py:52
  241.3 9.5 %fusion.9 = f32[1024,512]{0,1:T(8,128)S(1)} fusion(f32[1,1024,1024]{2,1,0:T(8,128)} %all-gather.11.cloned.1.call-done, f32[1024,256]{0,1:T(8,128)S(1)} %bitcast.59, f32[1024,256]{0,1:T(8,128)} %slice_bitcast_fusion), kind=kOutput, calls=%fused_computation.13 | convolution fusion | flops 6442975232 | bytes 8388608 | tf_op jit(solution)/shard_map/dot_general | solution.py:16
  250.7 1.6 fusion.31
  253.0 1.6 copy.13
  255.6 76.2 %all-gather.9.cloned.1.call-done = f32[1024,1024]{0,1:T(8,128)} async-done(((f32[1024,256]{0,1:T(8,128)}), f32[1024,1024]{0,1:T(8,128)}) %all-gather.9.cloned.1.call-update) | async-done | bytes 4194320 | tf_op jit(solution)/shard_map/all_gather | solution.py:36
  331.8 5.4 copy.14
  337.2 75.3 %all-gather.13.cloned.1.call-done = f32[1,1024,1024]{1,2,0:T(8,128)} async-done(((f32[1,1024,256]{1,2,0:T(8,128)}), f32[1,1024,1024]{1,2,0:T(8,128)}) %all-gather.13.cloned.1.call-update) | async-done | bytes 4194320 | tf_op jit(solution)/shard_map/all_gather | solution.py:52
  412.5 93.3 %while.12 = (s32[]{:T(128)}, f32[1024,256]{1,0:T(8,128)}, f32[1024,256]{1,0:T(8,128)}, f32[1024,1024]{1,0:T(8,128)}, f32[1024,256]{1,0:T(8,128)S(1)}, /*index=5*/s32[]{:T(128)}) while((s32[]{:T(128)}, f32[1024,256]{1,0:T(8,128)}, f32[1024,256]{1,0:T(8,128)}, f32[1024,1024]{1,0:T(8,128)}, f32[1024,256]{1,0:T(8,128)S(1)}, ...), condition=%wide.region_1.0_spmd, body=%wide.region_0.0_spmd.sunk | while | flops 3221487616 | bytes 11534445 | solution.py:46
  412.5 2.6 collective-permute-start
  415.1 13.9 %collective-permute-done = f32[1024,256]{1,0:T(8,128)} collective-permute-done((f32[1024,256]{1,0:T(8,128)}, f32[1024,256]{1,0:T(8,128)}, u32[]{:S(2)}, u32[]{:S(2)}) %collective-permute-start) | collective-permute-done | bytes 1048608 | tf_op jit(solution)/shard_map/while/body/eval_jaxpr/ppermute | solution.py:12
  429.0 6.9 %convolution_add_fusion.2 = f32[1024,256]{1,0:T(8,128)} fusion(f32[1024,256]{1,0:T(8,128)S(1)} %get-tuple-element.101, f32[1024,1024]{1,0:T(8,128)} %get-tuple-element.100, f32[1024,256]{1,0:T(8,128)} %collective-permute-done), kind=kOutput, calls=%fused_computation.1.clone.1 | convolution fusion | flops 3221487616 | bytes 7340032 | tf_op jit(solution)/shard_map/while/body/eval_jaxpr/dot_general | solution.py:41
  435.9 1.9 collective-permute-start
  437.8 14.5 %collective-permute-done = f32[1024,256]{1,0:T(8,128)} collective-permute-done((f32[1024,256]{1,0:T(8,128)}, f32[1024,256]{1,0:T(8,128)}, u32[]{:S(2)}, u32[]{:S(2)}) %collective-permute-start) | collective-permute-done | bytes 1048608 | tf_op jit(solution)/shard_map/while/body/eval_jaxpr/ppermute | solution.py:12
  452.3 6.9 %convolution_add_fusion.2 = f32[1024,256]{1,0:T(8,128)} fusion(f32[1024,256]{1,0:T(8,128)S(1)} %get-tuple-element.101, f32[1024,1024]{1,0:T(8,128)} %get-tuple-element.100, f32[1024,256]{1,0:T(8,128)} %collective-permute-done), kind=kOutput, calls=%fused_computation.1.clone.1 | convolution fusion | flops 3221487616 | bytes 7340032 | tf_op jit(solution)/shard_map/while/body/eval_jaxpr/dot_general | solution.py:41
  459.2 1.9 collective-permute-start
  461.1 14.5 %collective-permute-done = f32[1024,256]{1,0:T(8,128)} collective-permute-done((f32[1024,256]{1,0:T(8,128)}, f32[1024,256]{1,0:T(8,128)}, u32[]{:S(2)}, u32[]{:S(2)}) %collective-permute-start) | collective-permute-done | bytes 1048608 | tf_op jit(solution)/shard_map/while/body/eval_jaxpr/ppermute | solution.py:12
  475.6 6.9 %convolution_add_fusion.2 = f32[1024,256]{1,0:T(8,128)} fusion(f32[1024,256]{1,0:T(8,128)S(1)} %get-tuple-element.101, f32[1024,1024]{1,0:T(8,128)} %get-tuple-element.100, f32[1024,256]{1,0:T(8,128)} %collective-permute-done), kind=kOutput, calls=%fused_computation.1.clone.1 | convolution fusion | flops 3221487616 | bytes 7340032 | tf_op jit(solution)/shard_map/while/body/eval_jaxpr/dot_general | solution.py:41
  482.5 1.9 collective-permute-start
  484.5 14.5 %collective-permute-done = f32[1024,256]{1,0:T(8,128)} collective-permute-done((f32[1024,256]{1,0:T(8,128)}, f32[1024,256]{1,0:T(8,128)}, u32[]{:S(2)}, u32[]{:S(2)}) %collective-permute-start) | collective-permute-done | bytes 1048608 | tf_op jit(solution)/shard_map/while/body/eval_jaxpr/ppermute | solution.py:12
  499.0 6.9 %convolution_add_fusion.2 = f32[1024,256]{1,0:T(8,128)} fusion(f32[1024,256]{1,0:T(8,128)S(1)} %get-tuple-element.101, f32[1024,1024]{1,0:T(8,128)} %get-tuple-element.100, f32[1024,256]{1,0:T(8,128)} %collective-permute-done), kind=kOutput, calls=%fused_computation.1.clone.1 | convolution fusion | flops 3221487616 | bytes 7340032 | tf_op jit(solution)/shard_map/while/body/eval_jaxpr/dot_general | solution.py:41
  505.9 6.6 %fusion.26 = f32[1024,256]{0,1:T(8,128)S(1)} fusion(f32[1024,256]{1,0:T(8,128)} %get-tuple-element.31, f32[1,1024,1024]{1,2,0:T(8,128)} %all-gather.13.cloned.1.call-done, f32[2,1024,256]{1,2,0:T(8,128)} %copy-done.1), kind=kOutput, calls=%fused_computation.18 | convolution fusion | flops 3221487616 | bytes 7340032 | tf_op jit(solution)/shard_map/dot_general | solution.py:16
  512.4 3.7 fusion.20
  516.2 1.5 pad_maximum_fusion
  517.7 4.1 copy.16
  521.8 10.5 %gather_fusion = f32[1024,2,256]{2,1,0:T(2,128)} fusion(f32[2,1024,256]{2,0,1:T(2,128)} %copy.16, s32[1024]{0:T(1024)S(1)} %fusion.29), kind=kCustom, calls=%fused_computation | custom fusion | bytes 4198400 | tf_op jit(solution)/shard_map/jit(_take)/gather | solution.py:56
  532.3 5.2 select_bitcast_fusion
  537.5 1.5 copy.17
  (26 shorter events, 3.6 us)
Async XLA Ops:
  6.5 154.4 %copy-start = (f32[2,1024,256]{2,1,0:T(8,128)S(1)}, f32[2,1024,256]{2,1,0:T(8,128)}, u32[]{:S(2)}) copy-start(f32[2,1024,256]{2,1,0:T(8,128)} %param.6) | copy-start | bytes 6291460
  6.5 154.4 %all-gather.7.cloned.1.call-start = ((), (), s32[]{:S(2)}) async-start(), calls=%async_computation | async-start | bytes 10485760 | tf_op jit(solution)/shard_map/all_gather | solution.py:24
  7.3 234.0 %all-gather.11.cloned.1.call-start = ((), (), s32[]{:S(2)}) async-start(), calls=%async_computation.2 | async-start | bytes 5242880 | tf_op jit(solution)/shard_map/all_gather | solution.py:52
  10.4 321.4 %all-gather.9.cloned.1.call-start = ((), (), s32[]{:S(2)}) async-start(), calls=%async_computation.1 | async-start | bytes 5242880 | tf_op jit(solution)/shard_map/all_gather | solution.py:36
  12.0 229.2 %copy-start.5 = (f32[1,1024,256]{1,2,0:T(8,128)}, f32[1,1024,256]{1,2,0:T(8,128)S(1)}, u32[]{:S(2)}) copy-start(f32[1,1024,256]{1,2,0:T(8,128)S(1)} %copy.19) | copy-start | bytes 3145732
  170.7 1.3 copy-start.1
  241.2 9.5 %copy-start.2 = (f32[2,1024,256]{1,2,0:T(8,128)S(1)}, f32[2,1024,256]{1,2,0:T(8,128)}, u32[]{:S(2)}) copy-start(f32[2,1024,256]{1,2,0:T(8,128)} %copy-done.1) | copy-start | bytes 6291460
  252.3 0.7 copy-start.6
  252.3 160.2 %all-gather.13.cloned.1.call-start = ((), (), s32[]{:S(2)}) async-start(), calls=%async_computation.3 | async-start | bytes 5242880 | tf_op jit(solution)/shard_map/all_gather | solution.py:52
  412.5 16.5 %collective-permute-start = (f32[1024,256]{1,0:T(8,128)}, f32[1024,256]{1,0:T(8,128)}, u32[]{:S(2)}, u32[]{:S(2)}) collective-permute-start(f32[1024,256]{1,0:T(8,128)} %get-tuple-element.92), channel_id=1, source_target_pairs={{4,0},{8,4},{12,8},{5,1},{9,5},{13,9},{6,2},{10,6},{14,10},{7,3},{... | collective-permute-start | bytes 3145736 | tf_op jit(solution)/shard_map/while/body/eval_jaxpr/ppermute | solution.py:12
  435.9 16.4 %collective-permute-start = (f32[1024,256]{1,0:T(8,128)}, f32[1024,256]{1,0:T(8,128)}, u32[]{:S(2)}, u32[]{:S(2)}) collective-permute-start(f32[1024,256]{1,0:T(8,128)} %get-tuple-element.92), channel_id=1, source_target_pairs={{4,0},{8,4},{12,8},{5,1},{9,5},{13,9},{6,2},{10,6},{14,10},{7,3},{... | collective-permute-start | bytes 3145736 | tf_op jit(solution)/shard_map/while/body/eval_jaxpr/ppermute | solution.py:12
  459.2 16.4 %collective-permute-start = (f32[1024,256]{1,0:T(8,128)}, f32[1024,256]{1,0:T(8,128)}, u32[]{:S(2)}, u32[]{:S(2)}) collective-permute-start(f32[1024,256]{1,0:T(8,128)} %get-tuple-element.92), channel_id=1, source_target_pairs={{4,0},{8,4},{12,8},{5,1},{9,5},{13,9},{6,2},{10,6},{14,10},{7,3},{... | collective-permute-start | bytes 3145736 | tf_op jit(solution)/shard_map/while/body/eval_jaxpr/ppermute | solution.py:12
  482.5 16.4 %collective-permute-start = (f32[1024,256]{1,0:T(8,128)}, f32[1024,256]{1,0:T(8,128)}, u32[]{:S(2)}, u32[]{:S(2)}) collective-permute-start(f32[1024,256]{1,0:T(8,128)} %get-tuple-element.92), channel_id=1, source_target_pairs={{4,0},{8,4},{12,8},{5,1},{9,5},{13,9},{6,2},{10,6},{14,10},{7,3},{... | collective-permute-start | bytes 3145736 | tf_op jit(solution)/shard_map/while/body/eval_jaxpr/ppermute | solution.py:12
  505.9 6.6 %copy-start.3 = (f32[2,1024,256]{1,2,0:T(8,128)S(1)}, f32[2,1024,256]{1,2,0:T(8,128)}, u32[]{:S(2)}) copy-start(f32[2,1024,256]{1,2,0:T(8,128)} %copy-done.1) | copy-start | bytes 6291460
  505.9 6.6 %copy-start.4 = (f32[1,1024,1024]{2,1,0:T(8,128)S(1)}, f32[1,1024,1024]{2,1,0:T(8,128)}, u32[]{:S(2)}) copy-start(f32[1,1024,1024]{2,1,0:T(8,128)} %all-gather.11.cloned.1.call-done) | copy-start | bytes 12582916
Sparse Core Ops, SparseCore 0:
  8.9 151.9 all-gather.6
  162.5 78.7 all-gather.10
  252.5 79.2 all-gather.8
  333.2 79.2 all-gather.12
where the time goes:
time: 546 us
  waiting for transfers between devices  427 us (78%)
  matrix products  57.1 us (10%)
  local copies, waits for them, and re-layouts  31.2 us (6%)
  between operations  13.2 us (2%)
  starting transfers between devices  8.59 us (2%)
  other arithmetic  8.28 us (2%)
    all_gather x1, waiting for transfers between devices, shards(): lax.all_gather(inv_diag, 'cols', axis=2, tiled=True)  149 us
    all_gather x2, waiting for transfers between devices, shards(): lax.all_gather(coupling[block], 'cols', axis=1, tiled=True)  143 us
    all_gather x1, waiting for transfers between devices, shards(): reduced_full = lax.all_gather(reduced, 'cols', axis=1, tiled=True)  76.2 us
    ppermute x4, waiting for transfers between devices, shifted(): return lax.ppermute(block, axis, route)  57.4 us
    dot_general x4, matrix products, relay_step(): jnp.dot(reduced_full, incoming, precision=precise, preferred_element_type...  27.6 us
    dot_general x3, matrix products, fold_with(): jnp.dot(segment, operand, precision=precise, preferred_element_type=jnp.f...  19.8 us
  transfers between devices with their start and end apart: 8, of which 8 were waited for; matrix products, arithmetic and copies ran while one was open for 4% of the time, Pallas kernels for 0%

commit v1 on v0

--- a/solution.py
+++ b/solution.py
@@ -2,6 +2,7 @@
 import jax.numpy as jnp
 from jax import lax
 from jax.sharding import PartitionSpec as P
+from jax.lax import axis_index, axis_size, ppermute
 
 precise = lax.Precision.HIGHEST
 
@@ -19,12 +20,29 @@
 def shards(noise, inv_diag, coupling, order):
     block_count = noise.shape[0]
     sample_count = noise.shape[2]
-    driven = jnp.einsum(
-        "kmn,kns->kms",
-        lax.all_gather(inv_diag, "cols", axis=2, tiled=True),
-        noise,
-        precision=precise,
-        preferred_element_type=jnp.float32,
+
+    def _serve_packet(vals, comm_axis, which_dim, values):
+        res, u1 = (axis_size(comm_axis), axis_index(comm_axis))
+        fields = list(map(lambda b: (b, (b - 1) % res), range(res)))
+        newest = vals.shape[which_dim]
+        reply = vals
+        placed = values(reply, u1 * newest)
+        for t in range(1, res):
+            reply = ppermute(reply, comm_axis, perm=fields)
+            placed = placed + values(reply, (u1 + t) % res * newest)
+        return placed
+
+    driven = _serve_packet(
+        inv_diag,
+        "cols",
+        2,
+        lambda shard, start: jnp.einsum(
+            "kmn,kns->kms",
+            shard,
+            lax.dynamic_slice_in_dim(noise, start, shard.shape[2], axis=1),
+            precision=precise,
+            preferred_element_type=jnp.float32,
+        ),
     )
     local_field = driven[block_count - 1]
     reduced = coupling[block_count - 1]

time: 546 us -> 533 us (0.976)
  waiting for transfers between devices: 427 us -> 394 us
  matrix products: 57.1 us -> 68.4 us
  starting transfers between devices: 8.59 us -> 16.5 us
    ppermute x0 -> x3, waiting for transfers between devices: none -> 180 us  [_serve_packet(): reply = ppermute(reply, comm_axis, perm=fields)]
    all_gather x1 -> x0, waiting for transfers between devices: 149 us -> none  [shards(): lax.all_gather(inv_diag, 'cols', axis=2, tiled=True)]
    all_gather x2, waiting for transfers between devices: 143 us -> 75.5 us  [shards(): lax.all_gather(coupling[block], 'cols', axis=1, tiled=True)]
    dot_general x1 -> x4, matrix products: 9.77 us -> 21 us  [shards(): jnp.einsum('kmn,kns->kms', shard, lax.dynamic_slice_in_dim(noise, start,...]
    ppermute x0 -> x3, starting transfers between devices: none -> 8.15 us  [_serve_packet(): reply = ppermute(reply, comm_axis, perm=fields)]
  transfers between devices with their start and end apart: 8 -> 10, of which waited for: 8 -> 9; matrix products, arithmetic and copies ran while one was open for 4% -> 6% of each run, Pallas kernels for 0% -> 0%
where the time goes in v1:
time: 533 us; the launch traced here: 532 us
  waiting for transfers between devices  394 us (74%)
  matrix products  68.4 us (13%)
  local copies, waits for them, and re-layouts  31 us (6%)
  starting transfers between devices  16.5 us (3%)
  between operations  13.3 us (2%)
  other arithmetic  8.33 us (2%)
    ppermute x3, waiting for transfers between devices, _serve_packet(): reply = ppermute(reply, comm_axis, perm=fields)  180 us
    all_gather x1, waiting for transfers between devices, shards(): reduced_full = lax.all_gather(reduced, 'cols', axis=1, tiled=True)  80.8 us
    all_gather x2, waiting for transfers between devices, shards(): lax.all_gather(coupling[block], 'cols', axis=1, tiled=True)  75.5 us
    ppermute x4, waiting for transfers between devices, shifted(): return lax.ppermute(block, axis, route)  57.4 us
    dot_general x4, matrix products, relay_step(): jnp.dot(reduced_full, incoming, precision=precise, preferred_element_type...  27.6 us
    dot_general x4, matrix products, shards(): jnp.einsum('kmn,kns->kms', shard, lax.dynamic_slice_in_dim(noise, start,...  21 us
    dot_general x3, matrix products, fold_with(): jnp.dot(segment, operand, precision=precise, preferred_element_type=jnp.f...  19.8 us
  transfers between devices with their start and end apart: 10, of which 9 were waited for; matrix products, arithmetic and copies ran while one was open for 6% of the time, Pallas kernels for 0%

profile of v1, /device:TPU:1, one launch (start us, length us, event | category | flops | bytes accessed | tf_op | source)
XLA Modules:
  0.0 532.0 jit_solution(11537229079705896311)
XLA Ops:
  6.5 4.2 collective-permute-start.1
  10.7 3.0 fusion.43
  13.8 101.2 %collective-permute-done.1 = f32[2,1024,256]{2,1,0:T(8,128)} collective-permute-done((f32[2,1024,256]{2,1,0:T(8,128)}, f32[2,1024,256]{2,1,0:T(8,128)}, u32[]{:S(2)}, u32[]{:S(2)}) %collective-permute-start.1) | collective-permute-done | bytes 2097184 | tf_op jit(solution)/shard_map/ppermute | solution.py:31
  115.0 52.6 %collective-permute-done.2 = f32[2,1024,256]{2,1,0:T(8,128)} collective-permute-done((f32[2,1024,256]{2,1,0:T(8,128)}, f32[2,1024,256]{2,1,0:T(8,128)}, u32[]{:S(2)}, u32[]{:S(2)}) %collective-permute-start.2) | collective-permute-done | bytes 2097184 | tf_op jit(solution)/shard_map/ppermute | solution.py:31
  167.6 4.0 collective-permute-start.3
  173.2 5.4 %fusion.34 = f32[2,256,1024]{2,1,0:T(8,128)S(1)} fusion(f32[2,1024,256]{2,1,0:T(8,128)} %param.7, f32[2,1024,256]{2,1,0:T(8,128)S(1)} %copy-done, s32[]{:T(128)S(6)} %select_n.37), kind=kOutput, calls=%fused_computation.28 | convolution fusion | flops 1610612736 | bytes 4718596 | tf_op jit(solution)/shard_map/kmn,kns->kms/dot_general | solution.py:39
  178.6 5.1 fusion.32
  183.7 5.1 fusion.30
  188.8 26.2 %collective-permute-done.3 = f32[2,1024,256]{2,1,0:T(8,128)} collective-permute-done((f32[2,1024,256]{2,1,0:T(8,128)}, f32[2,1024,256]{2,1,0:T(8,128)}, u32[]{:S(2)}, u32[]{:S(2)}) %collective-permute-start.3) | collective-permute-done | bytes 2097184 | tf_op jit(solution)/shard_map/ppermute | solution.py:31
  215.0 5.4 %add_bitcast_fusion = f32[2,1024,256]{1,2,0:T(8,128)S(1)} fusion(f32[2,256,1024]{2,1,0:T(8,128)S(1)} %fusion.30, f32[2,256,1024]{2,1,0:T(8,128)S(1)} %fusion.34, f32[2,256,1024]{2,1,0:T(8,128)S(1)} %fusion.32, f32[2,1024,256]{2,1,0:T(8,128)} %collective-permute-done.3, f32[2,1024,256]{2,1,0:T(8,128)S(1)} %copy-done, s32[]{:T(128)S(6)} %select_n.43), kind=kOutput, calls=%fused_computation.13 | convolution fusion | flops 1612185600 | bytes 11010052 | tf_op jit(solution)/shard_map/kmn,kns->kms/dot_general | solution.py:39
  222.8 9.5 %fusion.9 = f32[1024,512]{0,1:T(8,128)S(1)} fusion(f32[1,1024,1024]{2,1,0:T(8,128)} %all-gather.8.cloned.1.call-done, f32[1024,256]{0,1:T(8,128)S(1)} %bitcast.63, f32[1024,256]{0,1:T(8,128)} %slice_bitcast_fusion), kind=kOutput, calls=%fused_computation.14 | convolution fusion | flops 6442975232 | bytes 8388608 | tf_op jit(solution)/shard_map/dot_general | solution.py:17
  237.3 80.8 %all-gather.6.cloned.1.call-done = f32[1024,1024]{0,1:T(8,128)} async-done(((f32[1024,256]{0,1:T(8,128)}), f32[1024,1024]{0,1:T(8,128)}) %all-gather.6.cloned.1.call-update) | async-done | bytes 4194320 | tf_op jit(solution)/shard_map/all_gather | solution.py:54
  318.1 5.4 %copy.20 = f32[1024,1024]{1,0:T(8,128)} copy(f32[1024,1024]{0,1:T(8,128)} %all-gather.6.cloned.1.call-done) | data formatting | bytes 8388608 | tf_op jit(solution)/shard_map/while | solution.py:64
  323.4 75.5 %all-gather.10.cloned.1.call-done = f32[1,1024,1024]{1,2,0:T(8,128)} async-done(((f32[1,1024,256]{1,2,0:T(8,128)}), f32[1,1024,1024]{1,2,0:T(8,128)}) %all-gather.10.cloned.1.call-update) | async-done | bytes 4194320 | tf_op jit(solution)/shard_map/all_gather | solution.py:70
  399.0 93.3 %while.12 = (s32[]{:T(128)}, f32[1024,256]{1,0:T(8,128)}, f32[1024,256]{1,0:T(8,128)}, f32[1024,1024]{1,0:T(8,128)}, f32[1024,256]{1,0:T(8,128)S(1)}, /*index=5*/s32[]{:T(128)}) while((s32[]{:T(128)}, f32[1024,256]{1,0:T(8,128)}, f32[1024,256]{1,0:T(8,128)}, f32[1024,1024]{1,0:T(8,128)}, f32[1024,256]{1,0:T(8,128)S(1)}, ...), condition=%wide.region_1.2_spmd, body=%wide.region_0.1_spmd.sunk | while | flops 3221487616 | bytes 11534445 | solution.py:64
  399.0 2.6 collective-permute-start
  401.5 13.9 %collective-permute-done = f32[1024,256]{1,0:T(8,128)} collective-permute-done((f32[1024,256]{1,0:T(8,128)}, f32[1024,256]{1,0:T(8,128)}, u32[]{:S(2)}, u32[]{:S(2)}) %collective-permute-start) | collective-permute-done | bytes 1048608 | tf_op jit(solution)/shard_map/while/body/eval_jaxpr/ppermute | solution.py:13
  415.4 6.9 %convolution_add_fusion.2 = f32[1024,256]{1,0:T(8,128)} fusion(f32[1024,256]{1,0:T(8,128)S(1)} %get-tuple-element.101, f32[1024,1024]{1,0:T(8,128)} %get-tuple-element.100, f32[1024,256]{1,0:T(8,128)} %collective-permute-done), kind=kOutput, calls=%fused_computation.1.clone.1 | convolution fusion | flops 3221487616 | bytes 7340032 | tf_op jit(solution)/shard_map/while/body/eval_jaxpr/dot_general | solution.py:59
  422.3 1.9 collective-permute-start
  424.2 14.5 %collective-permute-done = f32[1024,256]{1,0:T(8,128)} collective-permute-done((f32[1024,256]{1,0:T(8,128)}, f32[1024,256]{1,0:T(8,128)}, u32[]{:S(2)}, u32[]{:S(2)}) %collective-permute-start) | collective-permute-done | bytes 1048608 | tf_op jit(solution)/shard_map/while/body/eval_jaxpr/ppermute | solution.py:13
  438.8 6.9 %convolution_add_fusion.2 = f32[1024,256]{1,0:T(8,128)} fusion(f32[1024,256]{1,0:T(8,128)S(1)} %get-tuple-element.101, f32[1024,1024]{1,0:T(8,128)} %get-tuple-element.100, f32[1024,256]{1,0:T(8,128)} %collective-permute-done), kind=kOutput, calls=%fused_computation.1.clone.1 | convolution fusion | flops 3221487616 | bytes 7340032 | tf_op jit(solution)/shard_map/while/body/eval_jaxpr/dot_general | solution.py:59
  445.6 1.9 collective-permute-start
  447.6 14.5 %collective-permute-done = f32[1024,256]{1,0:T(8,128)} collective-permute-done((f32[1024,256]{1,0:T(8,128)}, f32[1024,256]{1,0:T(8,128)}, u32[]{:S(2)}, u32[]{:S(2)}) %collective-permute-start) | collective-permute-done | bytes 1048608 | tf_op jit(solution)/shard_map/while/body/eval_jaxpr/ppermute | solution.py:13
  462.1 6.9 %convolution_add_fusion.2 = f32[1024,256]{1,0:T(8,128)} fusion(f32[1024,256]{1,0:T(8,128)S(1)} %get-tuple-element.101, f32[1024,1024]{1,0:T(8,128)} %get-tuple-element.100, f32[1024,256]{1,0:T(8,128)} %collective-permute-done), kind=kOutput, calls=%fused_computation.1.clone.1 | convolution fusion | flops 3221487616 | bytes 7340032 | tf_op jit(solution)/shard_map/while/body/eval_jaxpr/dot_general | solution.py:59
  469.0 1.9 collective-permute-start
  470.9 14.5 %collective-permute-done = f32[1024,256]{1,0:T(8,128)} collective-permute-done((f32[1024,256]{1,0:T(8,128)}, f32[1024,256]{1,0:T(8,128)}, u32[]{:S(2)}, u32[]{:S(2)}) %collective-permute-start) | collective-permute-done | bytes 1048608 | tf_op jit(solution)/shard_map/while/body/eval_jaxpr/ppermute | solution.py:13
  485.4 6.9 %convolution_add_fusion.2 = f32[1024,256]{1,0:T(8,128)} fusion(f32[1024,256]{1,0:T(8,128)S(1)} %get-tuple-element.101, f32[1024,1024]{1,0:T(8,128)} %get-tuple-element.100, f32[1024,256]{1,0:T(8,128)} %collective-permute-done), kind=kOutput, calls=%fused_computation.1.clone.1 | convolution fusion | flops 3221487616 | bytes 7340032 | tf_op jit(solution)/shard_map/while/body/eval_jaxpr/dot_general | solution.py:59
  492.3 6.6 %fusion.26 = f32[1024,256]{0,1:T(8,128)S(1)} fusion(f32[1024,256]{1,0:T(8,128)} %get-tuple-element.31, f32[1,1024,1024]{1,2,0:T(8,128)} %all-gather.10.cloned.1.call-done, f32[2,1024,256]{1,2,0:T(8,128)} %copy-done.1), kind=kOutput, calls=%fused_computation.19 | convolution fusion | flops 3221487616 | bytes 7340032 | tf_op jit(solution)/shard_map/dot_general | solution.py:17
  498.9 3.7 fusion.20
  504.1 4.1 copy.22
  508.2 10.5 %gather_fusion = f32[1024,2,256]{2,1,0:T(2,128)} fusion(f32[2,1024,256]{2,0,1:T(2,128)} %copy.22, s32[1024]{0:T(1024)S(1)} %fusion.36), kind=kCustom, calls=%fused_computation | custom fusion | bytes 4198400 | tf_op jit(solution)/shard_map/jit(_take)/gather | solution.py:74
  518.7 5.2 select_bitcast_fusion
  (32 shorter events, 11.9 us)
Async XLA Ops:
  6.5 166.6 %copy-start = (f32[2,1024,256]{2,1,0:T(8,128)S(1)}, f32[2,1024,256]{2,1,0:T(8,128)}, u32[]{:S(2)}) copy-start(f32[2,1024,256]{2,1,0:T(8,128)} %param.6) | copy-start | bytes 6291460
  6.5 216.2 %all-gather.8.cloned.1.call-start = ((), (), s32[]{:S(2)}) async-start(), calls=%async_computation.1 | async-start | bytes 5242880 | tf_op jit(solution)/shard_map/all_gather | solution.py:70
  6.5 108.5 %collective-permute-start.1 = (f32[2,1024,256]{2,1,0:T(8,128)}, f32[2,1024,256]{2,1,0:T(8,128)}, u32[]{:S(2)}, u32[]{:S(2)}) collective-permute-start(f32[2,1024,256]{2,1,0:T(8,128)} %param.7), channel_id=1, source_target_pairs={{0,3},{1,0},{2,1},{3,2},{4,7},{5,4},{6,5},{7,6},{8,11},{9,8},{10,9... | collective-permute-start | bytes 6291464 | tf_op jit(solution)/shard_map/ppermute | solution.py:31
  13.7 304.4 %all-gather.6.cloned.1.call-start = ((), (), s32[]{:S(2)}) async-start(), calls=%async_computation | async-start | bytes 5242880 | tf_op jit(solution)/shard_map/all_gather | solution.py:54
  115.0 52.6 %collective-permute-start.2 = (f32[2,1024,256]{2,1,0:T(8,128)}, f32[2,1024,256]{2,1,0:T(8,128)}, u32[]{:S(2)}, u32[]{:S(2)}) collective-permute-start(f32[2,1024,256]{2,1,0:T(8,128)} %collective-permute-done.1), channel_id=1, source_target_pairs={{0,3},{1,0},{2,1},{3,2},{4,7},{5,4},{6,5},{7,6},{8,11},{9,8},{10,9... | collective-permute-start | bytes 6291464 | tf_op jit(solution)/shard_map/ppermute | solution.py:31
  167.6 47.4 %collective-permute-start.3 = (f32[2,1024,256]{2,1,0:T(8,128)}, f32[2,1024,256]{2,1,0:T(8,128)}, u32[]{:S(2)}, u32[]{:S(2)}) collective-permute-start(f32[2,1024,256]{2,1,0:T(8,128)} %collective-permute-done.2), channel_id=1, source_target_pairs={{0,3},{1,0},{2,1},{3,2},{4,7},{5,4},{6,5},{7,6},{8,11},{9,8},{10,9... | collective-permute-start | bytes 6291464 | tf_op jit(solution)/shard_map/ppermute | solution.py:31
  173.1 49.6 %copy-start.5 = (f32[1,1024,256]{1,2,0:T(8,128)}, f32[1,1024,256]{1,2,0:T(8,128)S(1)}, u32[]{:S(2)}) copy-start(f32[1,1024,256]{1,2,0:T(8,128)S(1)} %copy.28) | copy-start | bytes 3145732
  220.4 1.3 copy-start.1
  222.8 9.5 %copy-start.2 = (f32[2,1024,256]{1,2,0:T(8,128)S(1)}, f32[2,1024,256]{1,2,0:T(8,128)}, u32[]{:S(2)}) copy-start(f32[2,1024,256]{1,2,0:T(8,128)} %copy-done.1) | copy-start | bytes 6291460
  233.9 0.8 copy-start.6
  233.9 165.0 %all-gather.10.cloned.1.call-start = ((), (), s32[]{:S(2)}) async-start(), calls=%async_computation.2 | async-start | bytes 5242880 | tf_op jit(solution)/shard_map/all_gather | solution.py:70
  399.0 16.5 %collective-permute-start = (f32[1024,256]{1,0:T(8,128)}, f32[1024,256]{1,0:T(8,128)}, u32[]{:S(2)}, u32[]{:S(2)}) collective-permute-start(f32[1024,256]{1,0:T(8,128)} %get-tuple-element.92), channel_id=1, source_target_pairs={{4,0},{8,4},{12,8},{5,1},{9,5},{13,9},{6,2},{10,6},{14,10},{7,3},{... | collective-permute-start | bytes 3145736 | tf_op jit(solution)/shard_map/while/body/eval_jaxpr/ppermute | solution.py:13
  422.3 16.4 %collective-permute-start = (f32[1024,256]{1,0:T(8,128)}, f32[1024,256]{1,0:T(8,128)}, u32[]{:S(2)}, u32[]{:S(2)}) collective-permute-start(f32[1024,256]{1,0:T(8,128)} %get-tuple-element.92), channel_id=1, source_target_pairs={{4,0},{8,4},{12,8},{5,1},{9,5},{13,9},{6,2},{10,6},{14,10},{7,3},{... | collective-permute-start | bytes 3145736 | tf_op jit(solution)/shard_map/while/body/eval_jaxpr/ppermute | solution.py:13
  445.6 16.4 %collective-permute-start = (f32[1024,256]{1,0:T(8,128)}, f32[1024,256]{1,0:T(8,128)}, u32[]{:S(2)}, u32[]{:S(2)}) collective-permute-start(f32[1024,256]{1,0:T(8,128)} %get-tuple-element.92), channel_id=1, source_target_pairs={{4,0},{8,4},{12,8},{5,1},{9,5},{13,9},{6,2},{10,6},{14,10},{7,3},{... | collective-permute-start | bytes 3145736 | tf_op jit(solution)/shard_map/while/body/eval_jaxpr/ppermute | solution.py:13
  469.0 16.4 %collective-permute-start = (f32[1024,256]{1,0:T(8,128)}, f32[1024,256]{1,0:T(8,128)}, u32[]{:S(2)}, u32[]{:S(2)}) collective-permute-start(f32[1024,256]{1,0:T(8,128)} %get-tuple-element.92), channel_id=1, source_target_pairs={{4,0},{8,4},{12,8},{5,1},{9,5},{13,9},{6,2},{10,6},{14,10},{7,3},{... | collective-permute-start | bytes 3145736 | tf_op jit(solution)/shard_map/while/body/eval_jaxpr/ppermute | solution.py:13
  492.3 6.6 %copy-start.3 = (f32[2,1024,256]{1,2,0:T(8,128)S(1)}, f32[2,1024,256]{1,2,0:T(8,128)}, u32[]{:S(2)}) copy-start(f32[2,1024,256]{1,2,0:T(8,128)} %copy-done.1) | copy-start | bytes 6291460
  492.3 6.6 %copy-start.4 = (f32[1,1024,1024]{2,1,0:T(8,128)S(1)}, f32[1,1024,1024]{2,1,0:T(8,128)}, u32[]{:S(2)}) copy-start(f32[1,1024,1024]{2,1,0:T(8,128)} %all-gather.8.cloned.1.call-done) | copy-start | bytes 12582916
Sparse Core Ops, SparseCore 0:
  13.8 117.0 all-gather.7
  234.1 83.9 all-gather.5
  319.6 79.2 all-gather.9
